TPU v7x, 512 devices: a whole 4x8x8 slice. The times are simulated.
512 devices in a mesh: grp: 16 (over x, z_lo), ep: 32 (over y, z_hi, core).
Axes of the slice: x: 4, y: 8, z: 8 (z_hi: 2, z_lo: 4; z = z_hi * 4 + z_lo), core: 2. Of those that a mesh axis runs over, the one named last changes fastest.
Arguments:
- slot_hidden: bfloat16 [65536, 8, 768], P(('grp', 'ep')), may hold values from -6 to 6
- expert_ids: int32 [65536, 8], P(('grp', 'ep')), may hold values from 0 to 63, all different within a row; in each aligned block of 128 rows (0 to 127, 128 to 255, ...) at most 24 rows name the same one
- gate_fixed: int32 [65536, 8], P(('grp', 'ep')), may hold values from 1 to 65535
- master: float32 [64, 768, 2048], P('ep', 'grp'), may hold values from -6 to 6
- moment_one: bfloat16 [64, 768, 2048], P('ep', 'grp'), may hold values from -3 to 3
- moment_two: bfloat16 [64, 768, 2048], P('ep', 'grp'), may hold values from 0.0099487305 to 2
- gradient: bfloat16 [64, 768, 2048], P('ep', 'grp'), may hold values from -6 to 6
Outputs:
- mixed: bfloat16 [65536, 2048], P(('grp', 'ep'))
- backup: float32 [64, 768, 2048], P('ep', 'grp')
Inputs may be any that keep to these rules, and one draw needn't show every extreme that they name: `expert_ids`: in each aligned block of 128 rows (the rows of one device) no expert is named by more than 24 rows, a bound that some block reaches; the 8 experts of a row differ.
All inputs are finite; a program needn't handle non-finite values.
Results may differ from a plain program's by a relative error of at most 0.0057.
Values may be sent and summed in bfloat16 or wider, within the bound.
No kernel may reach another device: no remote copies, remote signals or barrier semaphores. Data moves between devices by JAX's collectives and lax.ppermute only.
A program may use at most 64 MiB of HBM per device.

v0:
```python
import math
import jax
import jax.numpy as jnp
from jax import lax
from jax.sharding import Mesh
from jax.sharding import PartitionSpec as P

GRP = ("grp_0", "grp_1")
GRP_EP = ("grp_0", "grp_1", "ep")
beta_one = 0.9
beta_two = 0.95
corr_one = 1.0 - 0.9**40
corr_two = 1.0 - 0.95**40
learn_rate = 0.05
decay_rate = 0.1
adam_eps = 1e-08
gate_unit = 65536.0


def from_behind(value, axis, steps):
    count = lax.axis_size(axis)
    pairs = [(source, (source + steps) % count) for source in range(count)]
    return lax.ppermute(value, axis, pairs)


def gather_axes(shard, axes, dim):
    if not axes:
        return shard
    nearer = lax.all_gather(shard, axes[-1], axis=dim, tiled=True)
    return gather_axes(nearer, axes[:-1], dim)


def cut_along(shard, dim, peers):
    dims = shard.shape
    tiles = shard.reshape(*dims[:dim], peers, dims[dim] // peers, *dims[dim + 1 :])
    return jnp.moveaxis(tiles, dim, 0)


def cut_rows(length, count):
    unit = 8 if length >= 8 * count else 1
    return [length // unit * k // count * unit for k in range(1, count)]


def laid_out(tiles, dim):
    dims = list(tiles.shape[1:])
    dims[dim] *= tiles.shape[0]
    return jnp.moveaxis(tiles, 0, dim).reshape(dims)


def exchange_in_pieces(shard, axis, pieces, split_dim, concat_dim):
    tiles = cut_along(shard, split_dim, lax.axis_size(axis))
    split_at = max(range(1, max(2, tiles.ndim - 1)), key=lambda d: tiles.shape[d])
    gathered = []
    for piece in jnp.split(tiles, cut_rows(tiles.shape[split_at], pieces), axis=split_at):
        if piece.size:
            gathered.append(lax.all_to_all(piece, axis, split_axis=0, concat_axis=0, tiled=True))
    return laid_out(jnp.concatenate(gathered, axis=split_at), concat_dim)


def adamw_step(master, moment_one, moment_two, gradient):
    widened = gradient.astype(jnp.float32)
    first_moment = beta_one * moment_one.astype(jnp.float32) + (1.0 - beta_one) * widened
    second_moment = beta_two * moment_two.astype(jnp.float32) + (1.0 - beta_two) * widened * widened
    return (
        first_moment / corr_one / (jnp.sqrt(second_moment / corr_two) + adam_eps)
        + decay_rate * master
    )


def slot_positions(ids_block, experts, capacity):
    onehot = (ids_block[:, None] == jnp.arange(experts, dtype=jnp.int32)[None, :]).astype(jnp.int32)
    before = jnp.cumsum(onehot, axis=0) - onehot
    slot_index = jnp.sum(before * onehot, axis=1)
    return ids_block * capacity + slot_index


def body(slot_hidden, expert_ids, gate_fixed, master, moment_one, moment_two, gradient):
    groups = lax.axis_size(GRP)
    ranks = lax.axis_size("ep")
    local_experts = master.shape[0]
    experts = local_experts * ranks
    tok_count, top_count, hidden_width = slot_hidden.shape
    width = master.shape[2]
    capacity = max(2, tok_count * top_count // experts + tok_count * top_count // (2 * experts))
    scaling = 1.0 / math.sqrt(hidden_width)
    step_dir = adamw_step(master, moment_one, moment_two, gradient)
    updated = master - learn_rate * step_dir
    partner_master = from_behind(master.astype(jnp.bfloat16), GRP, groups // 2).astype(master.dtype)
    partner_rest = from_behind((moment_one, moment_two, gradient), GRP, groups // 2)
    backup = adamw_step(partner_master, partner_rest[0], partner_rest[1], partner_rest[2])
    weights = updated.astype(jnp.bfloat16)
    pairs = tok_count * top_count
    positions = slot_positions(expert_ids.reshape(pairs), experts, capacity)
    outgoing = jnp.zeros((experts * capacity, hidden_width), jnp.bfloat16)
    outgoing = outgoing.at[positions].set(slot_hidden.reshape(pairs, hidden_width))
    outgoing = outgoing.reshape(experts, capacity, hidden_width)
    arrived = lax.all_to_all(outgoing, "ep", split_axis=0, concat_axis=1, tiled=True)
    gathered = gather_axes(weights, GRP, 1)
    product = jnp.einsum("erh,ehd->erd", arrived, gathered, preferred_element_type=jnp.float32)
    results = (product * scaling).astype(jnp.bfloat16)
    returned = exchange_in_pieces(results, "ep", 2, 1, 0)
    picked = returned.reshape(experts * capacity, width)[positions]
    factors = gate_fixed.reshape(pairs).astype(jnp.float32) / gate_unit
    weighted = (picked.astype(jnp.float32) * factors[:, None]).reshape(tok_count, top_count, width)
    mixed = jnp.sum(weighted, axis=1).astype(jnp.bfloat16)
    return (mixed, backup)


def solution(mesh):
    torus = Mesh(mesh.devices.reshape(4, 4, mesh.shape["ep"]), ("grp_0", "grp_1", "ep"))
    in_specs = (
        P(GRP_EP, None, None),
        P(GRP_EP, None),
        P(GRP_EP, None),
        P("ep", GRP, None),
        P("ep", GRP, None),
        P("ep", GRP, None),
        P("ep", GRP, None),
    )
    out_specs = (P(GRP_EP, None), P("ep", GRP, None))
    return jax.shard_map(body, mesh=torus, in_specs=in_specs, out_specs=out_specs, check_vma=False)
```

profile of v0, /device:TPU:21, one launch (start us, length us, event | category | flops | bytes accessed | tf_op | source)
XLA Modules:
  0.0 392.5 jit_solution(8593457974764892059)
XLA Ops:
  7.2 0.0 copy-start
  7.2 0.0 copy-start.4
  7.2 0.0 all-gather.3.cloned.1.call-start
  7.2 3.4 fusion.27
  10.6 0.0 all-gather.3.cloned.1.call-update
  10.6 0.0 all-gather.5.cloned.1.call-start
  10.7 49.0 %all-gather.3.cloned.1.call-done = bf16[2,192,2048]{2,1,0:T(8,128)(2,1)} async-done(((bf16[2,48,2048]{2,1,0:T(8,128)(2,1)}), bf16[2,192,2048]{2,1,0:T(8,128)(2,1)}) %all-gather.3.cloned.1.call-update) | async-done | bytes 1572880 | tf_op jit(solution)/shard_map/all_gather | solution.py:29
  59.7 0.0 all-gather.5.cloned.1.call-update
  59.7 0.0 copy-done.4
  59.8 0.1 copy.20
  59.9 0.1 eq.29
  59.9 0.1 eq.25
  60.1 18.0 %reduce-window.6 = s32[64,8,128]{2,1,0:T(8,128)S(1)} reduce-window(s32[64,8,128]{2,1,0:T(8,128)S(1)} %fusion.26, s32[]{:T(128)} %constant.8.clone.1), window={size=1x1x128 pad=0_0x0_0x127_0}, to_apply=%region_0.0 | reduce-window | flops 8323072 | bytes 524292 | tf_op jit(solution)/shard_map/reduce-window
  78.1 0.1 slice.10
  78.2 0.1 copy.22
  78.4 0.1 copy.23
  78.5 0.1 copy.19
  78.6 0.1 mul.75
  78.7 0.1 broadcast_add_fusion
  78.8 0.1 fusion.25
  78.9 0.0 copy-done
  78.9 6.9 %scatter_custom_fusion = bf16[1536,768]{1,0:T(8,128)(2,1)} fusion(s32[1024]{0:T(1024)S(1)} %bitcast.48, bf16[128,8,768]{2,1,0:T(8,128)(2,1)S(1)} %copy-done, bf16[]{:T(256)} %constant.14.clone.1), kind=kCustom, calls=%fused_computation.7 | custom fusion | bytes 3932162 | tf_op jit(solution)/shard_map/scatter | solution.py:95
  85.9 70.6 %all_to_all.28 = bf16[64,24,768]{2,1,0:T(8,128)(2,1)S(1)} all-to-all(bf16[64,24,768]{2,1,0:T(8,128)(2,1)} %bitcast.41), channel_id=1, replica_groups=mesh['grp_0'=4,'grp_1'=4,'ep'=32] {'ep'}, dimensions={0} | all-to-all | bytes 4718592 | tf_op jit(solution)/shard_map/all_to_all | solution.py:97
  156.4 1.6 copy.24
  158.0 7.9 %multiply_convert_fusion = bf16[2,768,2048]{2,1,0:T(8,128)(2,1)S(1)} fusion(bf16[2,768,768]{2,1,0:T(8,128)(2,1)} %bitcast.44, bf16[2,768,2048]{2,1,0:T(8,128)(2,1)} %all-gather.5.cloned.1.call-done), kind=kOutput, calls=%fused_computation.2 | convolution fusion | flops 4838129664 | bytes 14942208 | tf_op jit(solution)/shard_map/erh,ehd->erd/dot_general | solution.py:99
  165.9 1.1 copy.30
  167.0 0.0 copy-start.1
  167.0 2.7 copy-done.1
  169.7 1.5 split.8
  171.2 6.9 %all-to-all-start.1 = ((bf16[32,2,8,2048]{3,2,1,0:T(8,128)(2,1)}), bf16[32,2,8,2048]{3,2,1,0:T(8,128)(2,1)}, u32[]{:S(2)}, u32[]{:S(2)}) async-start(bf16[32,2,8,2048]{3,2,1,0:T(8,128)(2,1)} %split.8), calls=%async_computation.1 | async-start | bytes 4194304 | tf_op jit(solution)/shard_map/all_to_all | solution.py:56
  178.1 4.8 %split.9 = bf16[32,2,16,2048]{3,2,1,0:T(8,128)(2,1)} slice(bf16[32,2,24,2048]{3,2,1,0:T(8,128)(2,1)} %bitcast.40), slice={[0:32], [0:2], [8:24], [0:2048]} | slice | bytes 8388608 | tf_op jit(solution)/shard_map/split | solution.py:54
  183.0 45.7 %all-to-all-done.1 = bf16[32,2,8,2048]{3,2,1,0:T(8,128)(2,1)} async-done(((bf16[32,2,8,2048]{3,2,1,0:T(8,128)(2,1)}), bf16[32,2,8,2048]{3,2,1,0:T(8,128)(2,1)}, u32[]{:S(2)}, u32[]{:S(2)}) %all-to-all-start.1) | async-done | bytes 2097184 | tf_op jit(solution)/shard_map/all_to_all | solution.py:56
  228.6 14.3 %all-to-all-start.2 = ((bf16[32,2,16,2048]{3,2,1,0:T(8,128)(2,1)}), bf16[32,2,16,2048]{3,2,1,0:T(8,128)(2,1)}, u32[]{:S(2)}, u32[]{:S(2)}) async-start(bf16[32,2,16,2048]{3,2,1,0:T(8,128)(2,1)} %split.9), calls=%async_computation.2 | async-start | bytes 8388608 | tf_op jit(solution)/shard_map/all_to_all | solution.py:56
  242.9 0.0 copy-done.2
  242.9 1.9 collective-permute-start
  244.9 4.9 %collective-permute-start.1 = (bf16[2,48,2048]{2,1,0:T(8,128)(2,1)}, bf16[2,48,2048]{2,1,0:T(8,128)(2,1)S(1)}, u32[]{:S(2)}, u32[]{:S(2)}) collective-permute-start(bf16[2,48,2048]{2,1,0:T(8,128)(2,1)} %param.13), channel_id=1, source_target_pairs={{0,256},{32,288},{64,320},{96,352},{128,384},{160,416},{192,448},{... | collective-permute-start | bytes 1179656 | tf_op jit(solution)/shard_map/ppermute | solution.py:23
  249.8 1.9 collective-permute-start.2
  251.7 5.0 %collective-permute-start.3 = (bf16[2,48,2048]{2,1,0:T(8,128)(2,1)}, bf16[2,48,2048]{2,1,0:T(8,128)(2,1)S(1)}, u32[]{:S(2)}, u32[]{:S(2)}) collective-permute-start(bf16[2,48,2048]{2,1,0:T(8,128)(2,1)} %get-tuple-element.2), channel_id=1, source_target_pairs={{0,256},{32,288},{64,320},{96,352},{128,384},{160,416},{192,448},{... | collective-permute-start | bytes 1179656 | tf_op jit(solution)/shard_map/ppermute | solution.py:23
  256.8 0.7 copy.26
  257.5 24.6 %collective-permute-done.3 = bf16[2,48,2048]{2,1,0:T(8,128)(2,1)S(1)} collective-permute-done((bf16[2,48,2048]{2,1,0:T(8,128)(2,1)}, bf16[2,48,2048]{2,1,0:T(8,128)(2,1)S(1)}, u32[]{:S(2)}, u32[]{:S(2)}) %collective-permute-start.3) | collective-permute-done | bytes 393248 | tf_op jit(solution)/shard_map/ppermute | solution.py:23
  282.1 0.0 collective-permute-done
  282.1 0.0 collective-permute-done.1
  282.1 0.0 collective-permute-done.2
  282.1 1.5 fusion.13
  283.6 75.7 %all-to-all-done.2 = bf16[32,2,16,2048]{3,2,1,0:T(8,128)(2,1)} async-done(((bf16[32,2,16,2048]{3,2,1,0:T(8,128)(2,1)}), bf16[32,2,16,2048]{3,2,1,0:T(8,128)(2,1)}, u32[]{:S(2)}, u32[]{:S(2)}) %all-to-all-start.2) | async-done | bytes 4194336 | tf_op jit(solution)/shard_map/all_to_all | solution.py:56
  359.3 6.7 %pad_maximum_fusion = bf16[32,2,24,2048]{3,2,1,0:T(8,128)(2,1)} fusion(bf16[32,2,16,2048]{3,2,1,0:T(8,128)(2,1)} %all-to-all-done.2, bf16[32,2,8,2048]{3,2,1,0:T(8,128)(2,1)} %all-to-all-done.1), kind=kLoop, calls=%fused_computation.5 | loop fusion | flops 12582912 | bytes 12582912 | tf_op jit(solution)/shard_map/concatenate | solution.py:57
  366.0 12.4 %gather_fusion = bf16[1024,2048]{1,0:T(8,128)(2,1)} fusion(bf16[1536,2048]{1,0:T(8,128)(2,1)} %bitcast.38, s32[1024]{0:T(1024)S(1)} %broadcast_clamp_fusion), kind=kCustom, calls=%fused_computation | custom fusion | bytes 8392704 | tf_op jit(solution)/shard_map/gather | solution.py:102
  378.4 7.3 %fusion = bf16[128,2048]{1,0:T(8,128)(2,1)} fusion(bf16[1024,2048]{1,0:T(8,128)(2,1)} %gather_fusion, f32[128,8]{1,0:T(8,128)S(1)} %copy-done.3), kind=kLoop, calls=%fused_computation.4 | loop fusion | flops 6029312 | bytes 4722688 | tf_op jit(solution)/shard_map/reduce_sum | solution.py:105
  (13 shorter events, 0.1 us)
Async XLA Ops:
  7.2 71.8 %copy-start = (bf16[128,8,768]{2,1,0:T(8,128)(2,1)S(1)}, bf16[128,8,768]{2,1,0:T(8,128)(2,1)}, u32[]{:S(2)}) copy-start(bf16[128,8,768]{2,1,0:T(8,128)(2,1)} %param.7) | copy-start | bytes 4718596
  7.2 52.6 %copy-start.4 = (s32[128,8]{0,1:T(8,128)S(1)}, s32[128,8]{0,1:T(8,128)}, u32[]{:S(2)}) copy-start(s32[128,8]{0,1:T(8,128)} %param.8) | copy-start | bytes 12292
  7.2 52.5 %all-gather.3.cloned.1.call-start = ((), (), s32[]{:S(2)}) async-start(), calls=%async_computation.3 | async-start | bytes 1966080 | tf_op jit(solution)/shard_map/all_gather | solution.py:29
  10.6 147.4 %all-gather.5.cloned.1.call-start = ((), (), s32[]{:S(2)}) async-start(), calls=%async_computation.4 | async-start | bytes 7864320 | tf_op jit(solution)/shard_map/all_gather | solution.py:29
  167.0 2.7 copy-start.1
  171.2 57.4 %all-to-all-start.1 = ((bf16[32,2,8,2048]{3,2,1,0:T(8,128)(2,1)}), bf16[32,2,8,2048]{3,2,1,0:T(8,128)(2,1)}, u32[]{:S(2)}, u32[]{:S(2)}) async-start(bf16[32,2,8,2048]{3,2,1,0:T(8,128)(2,1)} %split.8), calls=%async_computation.1 | async-start | bytes 4194304 | tf_op jit(solution)/shard_map/all_to_all | solution.py:56
  182.9 60.0 %copy-start.2 = (bf16[2,48,2048]{2,1,0:T(8,128)(2,1)S(1)}, bf16[2,48,2048]{2,1,0:T(8,128)(2,1)}, u32[]{:S(2)}) copy-start(bf16[2,48,2048]{2,1,0:T(8,128)(2,1)} %param.11) | copy-start | bytes 1179652
  183.0 73.8 %copy-start.5 = (s32[128,8]{0,1:T(8,128)S(1)}, s32[128,8]{0,1:T(8,128)}, u32[]{:S(2)}) copy-start(s32[128,8]{0,1:T(8,128)} %param.9) | copy-start | bytes 12292
  228.6 130.7 %all-to-all-start.2 = ((bf16[32,2,16,2048]{3,2,1,0:T(8,128)(2,1)}), bf16[32,2,16,2048]{3,2,1,0:T(8,128)(2,1)}, u32[]{:S(2)}, u32[]{:S(2)}) async-start(bf16[32,2,16,2048]{3,2,1,0:T(8,128)(2,1)} %split.9), calls=%async_computation.2 | async-start | bytes 8388608 | tf_op jit(solution)/shard_map/all_to_all | solution.py:56
  242.9 39.1 %collective-permute-start = (bf16[2,48,2048]{2,1,0:T(8,128)(2,1)S(1)}, bf16[2,48,2048]{2,1,0:T(8,128)(2,1)S(1)}, u32[]{:S(2)}, u32[]{:S(2)}) collective-permute-start(bf16[2,48,2048]{2,1,0:T(8,128)(2,1)S(1)} %copy-done.2), channel_id=1, source_target_pairs={{0,256},{32,288},{64,320},{96,352},{128,384},{160,416},{192,448},{... | collective-permute-start | bytes 1179656 | tf_op jit(solution)/shard_map/ppermute | solution.py:23
  244.9 37.2 %collective-permute-start.1 = (bf16[2,48,2048]{2,1,0:T(8,128)(2,1)}, bf16[2,48,2048]{2,1,0:T(8,128)(2,1)S(1)}, u32[]{:S(2)}, u32[]{:S(2)}) collective-permute-start(bf16[2,48,2048]{2,1,0:T(8,128)(2,1)} %param.13), channel_id=1, source_target_pairs={{0,256},{32,288},{64,320},{96,352},{128,384},{160,416},{192,448},{... | collective-permute-start | bytes 1179656 | tf_op jit(solution)/shard_map/ppermute | solution.py:23
  249.8 32.3 %collective-permute-start.2 = (bf16[2,48,2048]{2,1,0:T(8,128)(2,1)}, bf16[2,48,2048]{2,1,0:T(8,128)(2,1)S(1)}, u32[]{:S(2)}, u32[]{:S(2)}) collective-permute-start(bf16[2,48,2048]{2,1,0:T(8,128)(2,1)} %param.12), channel_id=1, source_target_pairs={{0,256},{32,288},{64,320},{96,352},{128,384},{160,416},{192,448},{... | collective-permute-start | bytes 1179656 | tf_op jit(solution)/shard_map/ppermute | solution.py:23
  251.7 30.4 %collective-permute-start.3 = (bf16[2,48,2048]{2,1,0:T(8,128)(2,1)}, bf16[2,48,2048]{2,1,0:T(8,128)(2,1)S(1)}, u32[]{:S(2)}, u32[]{:S(2)}) collective-permute-start(bf16[2,48,2048]{2,1,0:T(8,128)(2,1)} %get-tuple-element.2), channel_id=1, source_target_pairs={{0,256},{32,288},{64,320},{96,352},{128,384},{160,416},{192,448},{... | collective-permute-start | bytes 1179656 | tf_op jit(solution)/shard_map/ppermute | solution.py:23
  366.0 12.4 %copy-start.3 = (f32[128,8]{1,0:T(8,128)S(1)}, f32[128,8]{1,0:T(8,128)}, u32[]{:S(2)}) copy-start(f32[128,8]{1,0:T(8,128)} %copy.26) | copy-start | bytes 12292
Sparse Core Ops, SparseCore 0:
  10.7 48.9 all-gather.2
  61.8 69.9 all-gather.4
where the time goes:
time: 393 us
  waiting for transfers between devices  195 us (50%)
  blocking collectives  70.6 us (18%)
  other arithmetic  37.1 us (9%)
  starting transfers between devices  35.1 us (9%)
  local copies, waits for them, and re-layouts  32.7 us (8%)
  between operations  14.2 us (4%)
  matrix products  7.85 us (2%)
    all_to_all x2, waiting for transfers between devices, exchange_in_pieces(): lax.all_to_all(piece, axis, split_axis=0, concat_axis=0, tiled=True)  121 us
    all_to_all x1, blocking collectives, body(): lax.all_to_all(outgoing, 'ep', split_axis=0, concat_axis=1, tiled=True)  70.6 us
    all_gather x2, waiting for transfers between devices, gather_axes(): nearer = lax.all_gather(shard, axes[-1], axis=dim, tiled=True)  49 us
    ppermute x4, waiting for transfers between devices, from_behind(): return lax.ppermute(value, axis, pairs)  24.6 us
    all_to_all x2, starting transfers between devices, exchange_in_pieces(): lax.all_to_all(piece, axis, split_axis=0, concat_axis=0, tiled=True)  21.2 us
    another operation x3, other arithmetic  18.2 us
    ppermute x4, starting transfers between devices, from_behind(): return lax.ppermute(value, axis, pairs)  13.8 us
    gather x1, local copies, waits for them, and re-layouts, body(): picked = returned.reshape(experts * capacity, width)[positions]  12.4 us
  transfers between devices with their start and end apart: 8, of which 4 were waited for; matrix products, arithmetic and copies ran while one was open for 9% of the time, Pallas kernels for 0%

commit v1 on v0

--- a/solution.py
+++ b/solution.py
@@ -94,7 +94,10 @@
     outgoing = jnp.zeros((experts * capacity, hidden_width), jnp.bfloat16)
     outgoing = outgoing.at[positions].set(slot_hidden.reshape(pairs, hidden_width))
     outgoing = outgoing.reshape(experts, capacity, hidden_width)
-    arrived = lax.all_to_all(outgoing, "ep", split_axis=0, concat_axis=1, tiled=True)
+    arrived = jnp.concatenate(
+        lax.all_to_all(jnp.stack(jnp.split(outgoing, lax.axis_size("ep"), axis=0)), "ep", 0, 0),
+        axis=1,
+    )
     gathered = gather_axes(weights, GRP, 1)
     product = jnp.einsum("erh,ehd->erd", arrived, gathered, preferred_element_type=jnp.float32)
     results = (product * scaling).astype(jnp.bfloat16)

time: 393 us -> 376 us (0.957)
  the two profiles are of different devices: /device:TPU:21 before, /device:TPU:19 now
where the time goes in v1:
time: 376 us
  waiting for transfers between devices  177 us (47%)
  blocking collectives  70.3 us (19%)
  other arithmetic  37.1 us (10%)
  local copies, waits for them, and re-layouts  34.9 us (9%)
  starting transfers between devices  33.8 us (9%)
  between operations  14.5 us (4%)
  matrix products  7.85 us (2%)
    all_to_all x2, waiting for transfers between devices, exchange_in_pieces(): lax.all_to_all(piece, axis, split_axis=0, concat_axis=0, tiled=True)  122 us
    all_to_all x1, blocking collectives, body(): lax.all_to_all(jnp.stack(jnp.split(outgoing, lax.axis_size('ep'), axis=0)...  70.3 us
    all_gather x2, waiting for transfers between devices, gather_axes(): nearer = lax.all_gather(shard, axes[-1], axis=dim, tiled=True)  30.4 us
    ppermute x4, waiting for transfers between devices, from_behind(): return lax.ppermute(value, axis, pairs)  24.6 us
    all_to_all x2, starting transfers between devices, exchange_in_pieces(): lax.all_to_all(piece, axis, split_axis=0, concat_axis=0, tiled=True)  19.9 us
    another operation x3, other arithmetic  18.2 us
    ppermute x4, starting transfers between devices, from_behind(): return lax.ppermute(value, axis, pairs)  13.8 us
    gather x1, local copies, waits for them, and re-layouts, body(): picked = returned.reshape(experts * capacity, width)[positions]  12.4 us
  transfers between devices with their start and end apart: 8, of which 4 were waited for; matrix products, arithmetic and copies ran while one was open for 10% of the time, Pallas kernels for 0%

profile of v1, /device:TPU:19, one launch (start us, length us, event | category | flops | bytes accessed | tf_op | source)
XLA Modules:
  0.0 375.7 jit_solution(15724488908924166134)
XLA Ops:
  7.2 0.0 copy-start
  7.2 0.0 all-gather.3.cloned.1.call-start
  7.2 3.4 fusion.29
  10.6 0.0 all-gather.3.cloned.1.call-update
  10.6 0.0 all-gather.5.cloned.1.call-start
  10.7 0.0 copy-done.5
  10.7 0.1 copy.19
  10.8 0.1 eq.29
  10.9 0.1 eq.25
  11.0 18.0 %reduce-window.6 = s32[64,8,128]{2,1,0:T(8,128)S(1)} reduce-window(s32[64,8,128]{2,1,0:T(8,128)S(1)} %fusion.26, s32[]{:T(128)} %constant.8.clone.1), window={size=1x1x128 pad=0_0x0_0x127_0}, to_apply=%region_0.0 | reduce-window | flops 8323072 | bytes 524292 | tf_op jit(solution)/shard_map/reduce-window
  29.0 0.1 slice.42
  29.1 0.1 copy.21
  29.3 0.1 copy.22
  29.4 30.4 %all-gather.3.cloned.1.call-done = bf16[2,192,2048]{2,1,0:T(8,128)(2,1)} async-done(((bf16[2,48,2048]{2,1,0:T(8,128)(2,1)}), bf16[2,192,2048]{2,1,0:T(8,128)(2,1)}) %all-gather.3.cloned.1.call-update) | async-done | bytes 1572880 | tf_op jit(solution)/shard_map/all_gather | solution.py:29
  59.8 0.0 all-gather.5.cloned.1.call-update
  59.8 0.1 copy.18
  59.9 0.1 mul.75
  60.0 0.1 broadcast_add_fusion
  60.2 0.1 fusion.25
  60.3 7.0 %scatter_custom_fusion = bf16[1536,768]{1,0:T(8,128)(2,1)} fusion(s32[1024]{0:T(1024)S(1)} %bitcast.108, bf16[128,8,768]{2,1,0:T(8,128)(2,1)S(1)} %copy-done, bf16[]{:T(256)} %constant.14.clone.1), kind=kCustom, calls=%fused_computation.7 | custom fusion | bytes 3932162 | tf_op jit(solution)/shard_map/scatter | solution.py:95
  67.2 1.5 fusion.28
  68.9 0.4 copy-done.2
  69.3 0.1 fusion.27
  69.7 70.3 %all_to_all.15 = bf16[32,2,24,768]{3,2,1,0:T(8,128)(2,1)S(1)} all-to-all(bf16[32,2,24,768]{3,2,1,0:T(8,128)(2,1)S(1)} %constant_dynamic-update-slice_fusion), channel_id=1, replica_groups=mesh['grp_0'=4,'grp_1'=4,'ep'=32] {'ep'}, dimensions={0} | all-to-all | bytes 4718592 | tf_op jit(solution)/shard_map/all_to_all | solution.py:98
  140.0 1.6 copy.23
  141.6 7.9 %multiply_convert_fusion = bf16[2,768,2048]{2,1,0:T(8,128)(2,1)S(1)} fusion(bf16[2,768,768]{2,1,0:T(8,128)(2,1)} %bitcast.72, bf16[2,768,2048]{2,1,0:T(8,128)(2,1)} %all-gather.5.cloned.1.call-done), kind=kOutput, calls=%fused_computation.2 | convolution fusion | flops 4838129664 | bytes 14942208 | tf_op jit(solution)/shard_map/erh,ehd->erd/dot_general | solution.py:102
  149.5 1.1 copy.29
  150.6 2.7 copy-done.1
  153.3 1.5 split.168
  154.8 7.0 %all-to-all-start.1 = ((bf16[32,2,8,2048]{3,2,1,0:T(8,128)(2,1)}), bf16[32,2,8,2048]{3,2,1,0:T(8,128)(2,1)}, u32[]{:S(2)}, u32[]{:S(2)}) async-start(bf16[32,2,8,2048]{3,2,1,0:T(8,128)(2,1)} %split.168), calls=%async_computation.1 | async-start | bytes 4194304 | tf_op jit(solution)/shard_map/all_to_all | solution.py:56
  161.8 4.9 %split.169 = bf16[32,2,16,2048]{3,2,1,0:T(8,128)(2,1)} slice(bf16[32,2,24,2048]{3,2,1,0:T(8,128)(2,1)} %bitcast.69), slice={[0:32], [0:2], [8:24], [0:2048]} | slice | bytes 8388608 | tf_op jit(solution)/shard_map/split | solution.py:54
  166.7 45.8 %all-to-all-done.1 = bf16[32,2,8,2048]{3,2,1,0:T(8,128)(2,1)} async-done(((bf16[32,2,8,2048]{3,2,1,0:T(8,128)(2,1)}), bf16[32,2,8,2048]{3,2,1,0:T(8,128)(2,1)}, u32[]{:S(2)}, u32[]{:S(2)}) %all-to-all-start.1) | async-done | bytes 2097184 | tf_op jit(solution)/shard_map/all_to_all | solution.py:56
  212.4 12.9 %all-to-all-start.2 = ((bf16[32,2,16,2048]{3,2,1,0:T(8,128)(2,1)}), bf16[32,2,16,2048]{3,2,1,0:T(8,128)(2,1)}, u32[]{:S(2)}, u32[]{:S(2)}) async-start(bf16[32,2,16,2048]{3,2,1,0:T(8,128)(2,1)} %split.169), calls=%async_computation.2 | async-start | bytes 8388608 | tf_op jit(solution)/shard_map/all_to_all | solution.py:56
  225.3 0.0 copy-done.3
  225.3 3.8 %collective-permute-start = (bf16[2,48,2048]{2,1,0:T(8,128)(2,1)S(1)}, bf16[2,48,2048]{2,1,0:T(8,128)(2,1)S(1)}, u32[]{:S(2)}, u32[]{:S(2)}) collective-permute-start(bf16[2,48,2048]{2,1,0:T(8,128)(2,1)S(1)} %copy-done.3), channel_id=1, source_target_pairs={{0,256},{32,288},{64,320},{96,352},{128,384},{160,416},{192,448},{... | collective-permute-start | bytes 1179656 | tf_op jit(solution)/shard_map/ppermute | solution.py:23
  229.2 3.0 collective-permute-start.1
  232.2 3.8 %collective-permute-start.2 = (bf16[2,48,2048]{2,1,0:T(8,128)(2,1)}, bf16[2,48,2048]{2,1,0:T(8,128)(2,1)S(1)}, u32[]{:S(2)}, u32[]{:S(2)}) collective-permute-start(bf16[2,48,2048]{2,1,0:T(8,128)(2,1)} %param.12), channel_id=1, source_target_pairs={{0,256},{32,288},{64,320},{96,352},{128,384},{160,416},{192,448},{... | collective-permute-start | bytes 1179656 | tf_op jit(solution)/shard_map/ppermute | solution.py:23
  236.0 3.1 collective-permute-start.3
  239.2 0.7 copy.25
  239.9 24.6 %collective-permute-done.3 = bf16[2,48,2048]{2,1,0:T(8,128)(2,1)S(1)} collective-permute-done((bf16[2,48,2048]{2,1,0:T(8,128)(2,1)}, bf16[2,48,2048]{2,1,0:T(8,128)(2,1)S(1)}, u32[]{:S(2)}, u32[]{:S(2)}) %collective-permute-start.3) | collective-permute-done | bytes 393248 | tf_op jit(solution)/shard_map/ppermute | solution.py:23
  264.5 0.0 collective-permute-done
  264.5 0.0 collective-permute-done.1
  264.5 0.0 collective-permute-done.2
  264.5 1.5 fusion.13
  266.0 76.4 %all-to-all-done.2 = bf16[32,2,16,2048]{3,2,1,0:T(8,128)(2,1)} async-done(((bf16[32,2,16,2048]{3,2,1,0:T(8,128)(2,1)}), bf16[32,2,16,2048]{3,2,1,0:T(8,128)(2,1)}, u32[]{:S(2)}, u32[]{:S(2)}) %all-to-all-start.2) | async-done | bytes 4194336 | tf_op jit(solution)/shard_map/all_to_all | solution.py:56
  342.4 6.7 %pad_maximum_fusion = bf16[32,2,24,2048]{3,2,1,0:T(8,128)(2,1)} fusion(bf16[32,2,16,2048]{3,2,1,0:T(8,128)(2,1)} %all-to-all-done.2, bf16[32,2,8,2048]{3,2,1,0:T(8,128)(2,1)} %all-to-all-done.1), kind=kLoop, calls=%fused_computation.5 | loop fusion | flops 12582912 | bytes 12582912 | tf_op jit(solution)/shard_map/concatenate | solution.py:57
  349.1 12.4 %gather_fusion = bf16[1024,2048]{1,0:T(8,128)(2,1)} fusion(bf16[1536,2048]{1,0:T(8,128)(2,1)} %bitcast.67, s32[1024]{0:T(1024)S(1)} %broadcast_clamp_fusion), kind=kCustom, calls=%fused_computation | custom fusion | bytes 8392704 | tf_op jit(solution)/shard_map/gather | solution.py:105
  361.5 7.3 %fusion = bf16[128,2048]{1,0:T(8,128)(2,1)} fusion(bf16[1024,2048]{1,0:T(8,128)(2,1)} %gather_fusion, f32[128,8]{1,0:T(8,128)S(1)} %copy-done.4), kind=kLoop, calls=%fused_computation.4 | loop fusion | flops 6029312 | bytes 4722688 | tf_op jit(solution)/shard_map/reduce_sum | solution.py:108
  (49 shorter events, 0.3 us)
Async XLA Ops:
  7.2 53.1 %copy-start = (bf16[128,8,768]{2,1,0:T(8,128)(2,1)S(1)}, bf16[128,8,768]{2,1,0:T(8,128)(2,1)}, u32[]{:S(2)}) copy-start(bf16[128,8,768]{2,1,0:T(8,128)(2,1)} %param.7) | copy-start | bytes 4718596
  7.2 3.5 copy-start.5
  7.2 52.6 %all-gather.3.cloned.1.call-start = ((), (), s32[]{:S(2)}) async-start(), calls=%async_computation.3 | async-start | bytes 1966080 | tf_op jit(solution)/shard_map/all_gather | solution.py:29
  10.6 131.0 %all-gather.5.cloned.1.call-start = ((), (), s32[]{:S(2)}) async-start(), calls=%async_computation.4 | async-start | bytes 7864320 | tf_op jit(solution)/shard_map/all_gather | solution.py:29
  67.2 2.1 copy-start.2
  150.6 2.7 copy-start.1
  154.8 57.6 %all-to-all-start.1 = ((bf16[32,2,8,2048]{3,2,1,0:T(8,128)(2,1)}), bf16[32,2,8,2048]{3,2,1,0:T(8,128)(2,1)}, u32[]{:S(2)}, u32[]{:S(2)}) async-start(bf16[32,2,8,2048]{3,2,1,0:T(8,128)(2,1)} %split.168), calls=%async_computation.1 | async-start | bytes 4194304 | tf_op jit(solution)/shard_map/all_to_all | solution.py:56
  166.6 58.7 %copy-start.3 = (bf16[2,48,2048]{2,1,0:T(8,128)(2,1)S(1)}, bf16[2,48,2048]{2,1,0:T(8,128)(2,1)}, u32[]{:S(2)}) copy-start(bf16[2,48,2048]{2,1,0:T(8,128)(2,1)} %param.11) | copy-start | bytes 1179652
  166.7 72.5 %copy-start.6 = (s32[128,8]{0,1:T(8,128)S(1)}, s32[128,8]{0,1:T(8,128)}, u32[]{:S(2)}) copy-start(s32[128,8]{0,1:T(8,128)} %param.9) | copy-start | bytes 12292
  212.4 130.0 %all-to-all-start.2 = ((bf16[32,2,16,2048]{3,2,1,0:T(8,128)(2,1)}), bf16[32,2,16,2048]{3,2,1,0:T(8,128)(2,1)}, u32[]{:S(2)}, u32[]{:S(2)}) async-start(bf16[32,2,16,2048]{3,2,1,0:T(8,128)(2,1)} %split.169), calls=%async_computation.2 | async-start | bytes 8388608 | tf_op jit(solution)/shard_map/all_to_all | solution.py:56
  225.3 39.1 %collective-permute-start = (bf16[2,48,2048]{2,1,0:T(8,128)(2,1)S(1)}, bf16[2,48,2048]{2,1,0:T(8,128)(2,1)S(1)}, u32[]{:S(2)}, u32[]{:S(2)}) collective-permute-start(bf16[2,48,2048]{2,1,0:T(8,128)(2,1)S(1)} %copy-done.3), channel_id=1, source_target_pairs={{0,256},{32,288},{64,320},{96,352},{128,384},{160,416},{192,448},{... | collective-permute-start | bytes 1179656 | tf_op jit(solution)/shard_map/ppermute | solution.py:23
  229.2 35.3 %collective-permute-start.1 = (bf16[2,48,2048]{2,1,0:T(8,128)(2,1)}, bf16[2,48,2048]{2,1,0:T(8,128)(2,1)S(1)}, u32[]{:S(2)}, u32[]{:S(2)}) collective-permute-start(bf16[2,48,2048]{2,1,0:T(8,128)(2,1)} %param.13), channel_id=1, source_target_pairs={{0,256},{32,288},{64,320},{96,352},{128,384},{160,416},{192,448},{... | collective-permute-start | bytes 1179656 | tf_op jit(solution)/shard_map/ppermute | solution.py:23
  232.2 32.3 %collective-permute-start.2 = (bf16[2,48,2048]{2,1,0:T(8,128)(2,1)}, bf16[2,48,2048]{2,1,0:T(8,128)(2,1)S(1)}, u32[]{:S(2)}, u32[]{:S(2)}) collective-permute-start(bf16[2,48,2048]{2,1,0:T(8,128)(2,1)} %param.12), channel_id=1, source_target_pairs={{0,256},{32,288},{64,320},{96,352},{128,384},{160,416},{192,448},{... | collective-permute-start | bytes 1179656 | tf_op jit(solution)/shard_map/ppermute | solution.py:23
  236.0 28.5 %collective-permute-start.3 = (bf16[2,48,2048]{2,1,0:T(8,128)(2,1)}, bf16[2,48,2048]{2,1,0:T(8,128)(2,1)S(1)}, u32[]{:S(2)}, u32[]{:S(2)}) collective-permute-start(bf16[2,48,2048]{2,1,0:T(8,128)(2,1)} %get-tuple-element.34), channel_id=1, source_target_pairs={{0,256},{32,288},{64,320},{96,352},{128,384},{160,416},{192,448},{... | collective-permute-start | bytes 1179656 | tf_op jit(solution)/shard_map/ppermute | solution.py:23
  349.1 12.4 %copy-start.4 = (f32[128,8]{1,0:T(8,128)S(1)}, f32[128,8]{1,0:T(8,128)}, u32[]{:S(2)}) copy-start(f32[128,8]{1,0:T(8,128)} %copy.25) | copy-start | bytes 12292
Sparse Core Ops, SparseCore 0:
  10.7 49.0 all-gather.2
  61.9 70.1 all-gather.4
